TPU v7x, 32 devices: a whole 2x2x4 slice. The times are simulated.
32 devices in a mesh: grad: 4 (over y, x), col: 8 (over z, core).
Axes of the slice: x: 2, y: 2, z: 4, core: 2. Of those that a mesh axis runs over, the one named last changes fastest.
Arguments:
- gradient: bfloat16 [16384, 53248], P(('grad', 'col'))
- test_matrix: bfloat16 [16384, 256], P(('grad', 'col')), may hold values from -6 to 6
Outputs:
- low_rank: float32 [16384, 256], P(('grad', 'col'))
- projector: float32 [53248, 256], P('col')
All inputs are finite; a program needn't handle non-finite values.
Results may differ from a plain program's by a relative error of at most 0.008.
Values may be sent and summed in bfloat16 or wider, within the bound.
No kernel may reach another device: no remote copies, remote signals or barrier semaphores. Data moves between devices by JAX's collectives and lax.ppermute only.
A program may use at most 256 MiB of HBM per device.

v0:
```python
import math
import jax
import jax.numpy as jnp
from jax import lax
from jax.sharding import PartitionSpec as P

FF = 53248
POWER = 2


def orthonormal(rows):
    partial_gram = lax.dot_general(
        rows,
        rows,
        (((0,), (0,)), ((), ())),
        precision=lax.Precision.HIGHEST,
        preferred_element_type=jnp.float32,
    )
    gram = lax.psum(partial_gram, ("grad", "col"))
    lower_factor = jnp.linalg.cholesky(gram)
    return lax.linalg.triangular_solve(
        lower_factor, rows, left_side=False, lower=True, transpose_a=True
    )


def shards(gradient, test_matrix):
    n_grad = lax.axis_size("grad")
    n_col = lax.axis_size("col")
    n_rows, n_ff = gradient.shape
    piece = n_ff // (n_col * n_grad)
    split = gradient.reshape(n_rows, n_col, n_grad, piece)
    blocks = lax.all_to_all(split, "grad", split_axis=2, concat_axis=0, tiled=True)
    blocks = blocks.reshape(n_grad * n_rows, n_col * piece)

    def sketch_of(row_piece):
        rows = lax.all_gather(row_piece, "grad", axis=0, tiled=True)
        partial = lax.dot_general(
            blocks, rows, (((0,), (0,)), ((), ())), preferred_element_type=jnp.float32
        )
        return lax.psum_scatter(partial, "col", scatter_dimension=0, tiled=True)

    sketch = sketch_of(test_matrix)
    for iteration in range(POWER + 1):
        basis_rows = orthonormal(sketch)
        basis_bf = lax.all_gather(basis_rows.astype(jnp.bfloat16), "col", axis=0, tiled=True)
        reduced = lax.psum_scatter(
            jnp.dot(blocks, basis_bf, preferred_element_type=jnp.float32),
            "grad",
            scatter_dimension=0,
            tiled=True,
        )
        if iteration < POWER:
            sketch = sketch_of(reduced.astype(jnp.bfloat16))
    projector = lax.all_gather(basis_rows * math.sqrt(FF), "grad", axis=0, tiled=True)
    return (reduced, projector)


def solution(mesh):
    return jax.shard_map(
        shards,
        mesh=mesh,
        in_specs=(P(("grad", "col"), None), P(("grad", "col"), None)),
        out_specs=(P(("grad", "col"), None), P("col", None)),
        check_vma=False,
    )
```

profile of v0, /device:TPU:0, one launch (start us, length us, event | category | flops | bytes accessed | tf_op | source)
XLA Modules:
  0.0 2358.2 jit_solution(13075918259095874959)
XLA Ops:
  7.2 73.2 %reshape.28 = bf16[512,8,4,1664]{3,2,1,0:T(4,128)(2,1)} reshape(bf16[512,53248]{1,0:T(8,128)(2,1)} %param.5) | data formatting | bytes 109051904 | tf_op jit(solution)/shard_map/reshape | solution.py:31
  80.4 36.6 %copy.12 = bf16[512,8,4,1664]{3,1,0,2:T(8,128)(2,1)} copy(bf16[512,8,4,1664]{3,2,1,0:T(4,128)(2,1)} %reshape.28) | data formatting | bytes 109051904 | tf_op jit(solution)/shard_map/reshape | solution.py:31
  117.0 12.1 all-to-all-start
  129.8 596.0 %all-to-all-done = bf16[512,8,4,1664]{3,1,0,2:T(8,128)(2,1)} async-done(((bf16[512,8,4,1664]{3,1,0,2:T(8,128)(2,1)}), bf16[512,8,4,1664]{3,1,0,2:T(8,128)(2,1)}, u32[]{:S(2)}, u32[]{:S(2)}) %all-to-all-start) | async-done | bytes 54525984 | tf_op jit(solution)/shard_map/all_to_all | solution.py:32
  725.8 36.6 %copy.24 = bf16[256,8,8,1664]{3,1,2,0:T(8,128)(2,1)} copy(bf16[256,8,8,1664]{3,2,1,0:T(8,128)(2,1)} %bitcast.37) | data formatting | bytes 109051904
  762.4 28.2 %fusion.37 = f32[13312,256]{1,0:T(8,128)} fusion(bf16[2048,13312]{1,0:T(8,128)(2,1)} %bitcast.131, bf16[2048,256]{1,0:T(8,128)(2,1)} %all-gather.8.cloned.1.call-done), kind=kOutput, calls=%fused_computation.90 | convolution fusion | flops 13958643712 | bytes 69206016 | tf_op jit(solution)/shard_map/dot_general | solution.py:37
  790.7 139.5 %reduce-scatter.7.cloned.1.call-done = f32[1664,256]{1,0:T(8,128)} async-done(((f32[13312,256]{1,0:T(8,128)}), f32[1664,256]{1,0:T(8,128)}) %reduce-scatter.7.cloned.1.call-update) | async-done | bytes 1703952 | tf_op jit(solution)/shard_map/reduce_scatter | solution.py:40
  930.2 5.9 fusion.38
  936.6 124.7 %all-reduce.5.cloned.1.call-done = f32[256,256]{0,1:T(8,128)} async-done(((f32[256,256]{0,1:T(8,128)}), f32[256,256]{0,1:T(8,128)}) %all-reduce.5.cloned.1.call-update) | async-done | bytes 262160 | tf_op jit(solution)/shard_map/psum | solution.py:19
  1063.4 11.7 cholesky.172
  1075.2 9.8 custom-call.15
  1085.5 11.7 cholesky.189
  1099.3 4.1 while.6
  1103.5 19.7 custom-call.16
  1127.7 68.2 %all-gather.10.cloned.1.call-done = bf16[13312,256]{0,1:T(8,128)(2,1)} async-done(((bf16[1664,256]{0,1:T(8,128)(2,1)}), bf16[13312,256]{0,1:T(8,128)(2,1)}) %all-gather.10.cloned.1.call-update) | async-done | bytes 6815760 | tf_op jit(solution)/shard_map/all_gather | solution.py:45
  1195.9 24.2 %convolution_bitcast_fusion.4 = f32[2048,256]{0,1:T(8,128)} fusion(bf16[13312,256]{0,1:T(8,128)(2,1)} %all-gather.10.cloned.1.call-done, bf16[2048,13312]{1,0:T(8,128)(2,1)} %bitcast.132), kind=kOutput, calls=%fused_computation.10 | convolution fusion | flops 13958643712 | bytes 63438848 | tf_op jit(solution)/shard_map/dot_general | solution.py:47
  1220.2 33.9 %reduce-scatter.9.cloned.1.call-done = f32[512,256]{0,1:T(8,128)} async-done(((f32[2048,256]{0,1:T(8,128)}), f32[512,256]{0,1:T(8,128)}) %reduce-scatter.9.cloned.1.call-update) | async-done | bytes 524304 | tf_op jit(solution)/shard_map/reduce_scatter | solution.py:46
  1254.1 1.8 convert_element_type.16
  1255.9 26.8 %all-gather.12.cloned.1.call-done = bf16[2048,256]{0,1:T(8,128)(2,1)} async-done(((bf16[512,256]{0,1:T(8,128)(2,1)}), bf16[2048,256]{0,1:T(8,128)(2,1)}) %all-gather.12.cloned.1.call-update) | async-done | bytes 1048592 | tf_op jit(solution)/shard_map/all_gather | solution.py:36
  1282.7 28.3 %convolution_bitcast_fusion.1 = f32[13312,256]{0,1:T(8,128)} fusion(bf16[2048,256]{0,1:T(8,128)(2,1)} %all-gather.12.cloned.1.call-done, bf16[2048,13312]{1,0:T(8,128)(2,1)} %bitcast.133), kind=kOutput, calls=%fused_computation.7 | convolution fusion | flops 13958643712 | bytes 69206016 | tf_op jit(solution)/shard_map/dot_general | solution.py:37
  1311.3 138.9 %reduce-scatter.11.cloned.1.call-done = f32[1664,256]{0,1:T(8,128)} async-done(((f32[13312,256]{0,1:T(8,128)}), f32[1664,256]{0,1:T(8,128)}) %reduce-scatter.11.cloned.1.call-update) | async-done | bytes 1703952 | tf_op jit(solution)/shard_map/reduce_scatter | solution.py:40
  1450.3 4.7 fusion.39
  1455.0 126.4 %all-reduce.7.cloned.1.call-done = f32[256,256]{0,1:T(8,128)} async-done(((f32[256,256]{0,1:T(8,128)}), f32[256,256]{0,1:T(8,128)}) %all-reduce.7.cloned.1.call-update) | async-done | bytes 262160 | tf_op jit(solution)/shard_map/psum | solution.py:19
  1583.5 11.7 cholesky.206
  1595.3 9.8 custom-call.17
  1605.6 11.7 cholesky.223
  1620.0 4.4 while.7
  1624.3 19.7 custom-call.18
  1647.8 68.2 %all-gather.14.cloned.1.call-done = bf16[13312,256]{0,1:T(8,128)(2,1)} async-done(((bf16[1664,256]{0,1:T(8,128)(2,1)}), bf16[13312,256]{0,1:T(8,128)(2,1)}) %all-gather.14.cloned.1.call-update) | async-done | bytes 6815760 | tf_op jit(solution)/shard_map/all_gather | solution.py:45
  1716.0 24.3 %convolution_bitcast_fusion.3 = f32[2048,256]{0,1:T(8,128)} fusion(bf16[13312,256]{0,1:T(8,128)(2,1)} %all-gather.14.cloned.1.call-done, bf16[2048,13312]{1,0:T(8,128)(2,1)} %bitcast.134), kind=kOutput, calls=%fused_computation.9 | convolution fusion | flops 13958643712 | bytes 63438848 | tf_op jit(solution)/shard_map/dot_general | solution.py:47
  1740.3 33.9 %reduce-scatter.13.cloned.1.call-done = f32[512,256]{0,1:T(8,128)} async-done(((f32[2048,256]{0,1:T(8,128)}), f32[512,256]{0,1:T(8,128)}) %reduce-scatter.13.cloned.1.call-update) | async-done | bytes 524304 | tf_op jit(solution)/shard_map/reduce_scatter | solution.py:46
  1774.2 1.8 convert_element_type.18
  1776.0 27.0 %all-gather.16.cloned.1.call-done = bf16[2048,256]{0,1:T(8,128)(2,1)} async-done(((bf16[512,256]{0,1:T(8,128)(2,1)}), bf16[2048,256]{0,1:T(8,128)(2,1)}) %all-gather.16.cloned.1.call-update) | async-done | bytes 1048592 | tf_op jit(solution)/shard_map/all_gather | solution.py:36
  1803.0 28.3 %convolution_bitcast_fusion = f32[13312,256]{0,1:T(8,128)} fusion(bf16[2048,256]{0,1:T(8,128)(2,1)} %all-gather.16.cloned.1.call-done, bf16[2048,13312]{1,0:T(8,128)(2,1)} %bitcast.135), kind=kOutput, calls=%fused_computation.6 | convolution fusion | flops 13958643712 | bytes 69206016 | tf_op jit(solution)/shard_map/dot_general | solution.py:37
  1831.6 139.0 %reduce-scatter.15.cloned.1.call-done = f32[1664,256]{0,1:T(8,128)} async-done(((f32[13312,256]{0,1:T(8,128)}), f32[1664,256]{0,1:T(8,128)}) %reduce-scatter.15.cloned.1.call-update) | async-done | bytes 1703952 | tf_op jit(solution)/shard_map/reduce_scatter | solution.py:40
  1970.5 4.7 fusion.40
  1975.3 126.4 %all-reduce.9.cloned.1.call-done = f32[256,256]{0,1:T(8,128)} async-done(((f32[256,256]{0,1:T(8,128)}), f32[256,256]{0,1:T(8,128)}) %all-reduce.9.cloned.1.call-update) | async-done | bytes 262160 | tf_op jit(solution)/shard_map/psum | solution.py:19
  2103.8 11.7 cholesky.240
  2115.5 9.8 custom-call.19
  2125.8 11.7 cholesky.257
  2140.2 4.2 while.8
  2144.4 19.7 custom-call.20
  2169.3 66.8 %all-gather.18.cloned.1.call-done = bf16[13312,256]{0,1:T(8,128)(2,1)} async-done(((bf16[1664,256]{0,1:T(8,128)(2,1)}), bf16[13312,256]{0,1:T(8,128)(2,1)}) %all-gather.18.cloned.1.call-update) | async-done | bytes 6815760 | tf_op jit(solution)/shard_map/all_gather | solution.py:45
  2236.1 25.5 %convolution_bitcast_fusion.2 = f32[2048,256]{0,1:T(8,128)} fusion(bf16[13312,256]{0,1:T(8,128)(2,1)} %all-gather.18.cloned.1.call-done, bf16[2048,13312]{1,0:T(8,128)(2,1)} %bitcast.136), kind=kOutput, calls=%fused_computation.8 | convolution fusion | flops 13958643712 | bytes 63438848 | tf_op jit(solution)/shard_map/dot_general | solution.py:47
  2261.7 49.8 %all-gather.20.cloned.1.call-done = f32[6656,256]{0,1:T(8,128)} async-done(((f32[1664,256]{0,1:T(8,128)}), f32[6656,256]{0,1:T(8,128)}) %all-gather.20.cloned.1.call-update) | async-done | bytes 6815760 | tf_op jit(solution)/shard_map/all_gather | solution.py:54
  2311.4 8.1 copy.20
  2319.5 30.0 %reduce-scatter.17.cloned.1.call-done = f32[512,256]{0,1:T(8,128)} async-done(((f32[2048,256]{0,1:T(8,128)}), f32[512,256]{0,1:T(8,128)}) %reduce-scatter.17.cloned.1.call-update) | async-done | bytes 524304 | tf_op jit(solution)/shard_map/reduce_scatter | solution.py:46
  2349.4 2.0 copy.19
  (107 shorter events, 38.7 us)
Async XLA Ops:
  117.0 608.8 %all-to-all-start = ((bf16[512,8,4,1664]{3,1,0,2:T(8,128)(2,1)}), bf16[512,8,4,1664]{3,1,0,2:T(8,128)(2,1)}, u32[]{:S(2)}, u32[]{:S(2)}) async-start(bf16[512,8,4,1664]{3,1,0,2:T(8,128)(2,1)} %copy.12), calls=%async_computation | async-start | bytes 109051904 | tf_op jit(solution)/shard_map/all_to_all | solution.py:32
  129.0 633.4 %all-gather.8.cloned.1.call-start = ((), (), s32[]{:S(2)}) async-start(), calls=%async_computation.7 | async-start | bytes 1310720 | tf_op jit(solution)/shard_map/all_gather | solution.py:36
  129.8 800.4 %reduce-scatter.7.cloned.1.call-start = ((), (), s32[]{:S(2)}) async-start(), calls=%async_computation.8 | async-start | bytes 15335424 | tf_op jit(solution)/shard_map/reduce_scatter | solution.py:40
  790.6 270.7 %all-reduce.5.cloned.1.call-start = ((), (), s32[]{:S(2)}) async-start(), calls=%async_computation.9 | async-start | bytes 524288 | tf_op jit(solution)/shard_map/psum | solution.py:19
  936.1 187.1 %copy-start = (f32[1664,256]{1,0:T(8,128)S(1)}, f32[1664,256]{1,0:T(8,128)}, u32[]{:S(2)}) copy-start(f32[1664,256]{1,0:T(8,128)} %reduce-scatter.7.cloned.1.call-done) | copy-start | bytes 5111812
  936.1 259.7 %all-gather.10.cloned.1.call-start = ((), (), s32[]{:S(2)}) async-start(), calls=%async_computation.10 | async-start | bytes 7667712 | tf_op jit(solution)/shard_map/all_gather | solution.py:45
  1127.6 126.4 %reduce-scatter.9.cloned.1.call-start = ((), (), s32[]{:S(2)}) async-start(), calls=%async_computation.11 | async-start | bytes 2621440 | tf_op jit(solution)/shard_map/reduce_scatter | solution.py:46
  1220.1 62.6 %all-gather.12.cloned.1.call-start = ((), (), s32[]{:S(2)}) async-start(), calls=%async_computation.12 | async-start | bytes 1310720 | tf_op jit(solution)/shard_map/all_gather | solution.py:36
  1255.9 194.4 %reduce-scatter.11.cloned.1.call-start = ((), (), s32[]{:S(2)}) async-start(), calls=%async_computation.13 | async-start | bytes 15335424 | tf_op jit(solution)/shard_map/reduce_scatter | solution.py:40
  1311.1 270.3 %all-reduce.7.cloned.1.call-start = ((), (), s32[]{:S(2)}) async-start(), calls=%async_computation.14 | async-start | bytes 524288 | tf_op jit(solution)/shard_map/psum | solution.py:19
  1455.0 189.1 %copy-start.2 = (f32[1664,256]{0,1:T(8,128)S(1)}, f32[1664,256]{0,1:T(8,128)}, u32[]{:S(2)}) copy-start(f32[1664,256]{0,1:T(8,128)} %reduce-scatter.11.cloned.1.call-done) | copy-start | bytes 5111812
  1455.0 261.0 %all-gather.14.cloned.1.call-start = ((), (), s32[]{:S(2)}) async-start(), calls=%async_computation.15 | async-start | bytes 7667712 | tf_op jit(solution)/shard_map/all_gather | solution.py:45
  1647.8 126.4 %reduce-scatter.13.cloned.1.call-start = ((), (), s32[]{:S(2)}) async-start(), calls=%async_computation.16 | async-start | bytes 2621440 | tf_op jit(solution)/shard_map/reduce_scatter | solution.py:46
  1740.3 62.7 %all-gather.16.cloned.1.call-start = ((), (), s32[]{:S(2)}) async-start(), calls=%async_computation.17 | async-start | bytes 1310720 | tf_op jit(solution)/shard_map/all_gather | solution.py:36
  1776.0 194.6 %reduce-scatter.15.cloned.1.call-start = ((), (), s32[]{:S(2)}) async-start(), calls=%async_computation.18 | async-start | bytes 15335424 | tf_op jit(solution)/shard_map/reduce_scatter | solution.py:40
  1831.4 270.3 %all-reduce.9.cloned.1.call-start = ((), (), s32[]{:S(2)}) async-start(), calls=%async_computation.19 | async-start | bytes 524288 | tf_op jit(solution)/shard_map/psum | solution.py:19
  1975.2 188.9 %copy-start.1 = (f32[1664,256]{0,1:T(8,128)S(1)}, f32[1664,256]{0,1:T(8,128)}, u32[]{:S(2)}) copy-start(f32[1664,256]{0,1:T(8,128)} %reduce-scatter.15.cloned.1.call-done) | copy-start | bytes 5111812
  1975.2 260.9 %all-gather.18.cloned.1.call-start = ((), (), s32[]{:S(2)}) async-start(), calls=%async_computation.20 | async-start | bytes 7667712 | tf_op jit(solution)/shard_map/all_gather | solution.py:45
  2167.9 143.5 %all-gather.20.cloned.1.call-start = ((), (), s32[]{:S(2)}) async-start(), calls=%async_computation.22 | async-start | bytes 8519680 | tf_op jit(solution)/shard_map/all_gather | solution.py:54
  2169.3 180.2 %reduce-scatter.17.cloned.1.call-start = ((), (), s32[]{:S(2)}) async-start(), calls=%async_computation.21 | async-start | bytes 2621440 | tf_op jit(solution)/shard_map/reduce_scatter | solution.py:46
Sparse Core Ops, SparseCore 0:
  131.7 318.6 all-gather.7
  790.8 139.4 reduce-scatter.6
  936.3 124.9 all-reduce.4
  1127.7 68.0 all-gather.9
  1220.2 33.7 reduce-scatter.8
  1256.3 26.3 all-gather.11
  1311.2 139.0 reduce-scatter.10
  1456.3 125.0 all-reduce.6
  1647.9 68.0 all-gather.13
  1740.4 33.7 reduce-scatter.12
  1776.6 26.3 all-gather.15
  1831.5 139.0 reduce-scatter.14
  1976.6 125.0 all-reduce.8
  2168.0 68.0 all-gather.17
  2238.4 72.9 all-gather.19
  2314.2 35.1 reduce-scatter.16
where the time goes:
time: 2370 us; the launch traced here: 2360 us
  waiting for transfers between devices  1800 us (76%)
  matrix products  184 us (8%)
  other arithmetic  173 us (7%)
  local copies, waits for them, and re-layouts  172 us (7%)
    all_to_all x1, waiting for transfers between devices, shards(): lax.all_to_all(split, 'grad', split_axis=2, concat_axis=0, tiled=True)  596 us
    reduce_scatter x3, waiting for transfers between devices, sketch_of(): return lax.psum_scatter(partial, 'col', scatter_dimension=0, tiled=True)  417 us
    psum x3, waiting for transfers between devices, orthonormal(): gram = lax.psum(partial_gram, ('grad', 'col'))  377 us
    all_gather x3, waiting for transfers between devices, shards(): lax.all_gather(basis_rows.astype(jnp.bfloat16), 'col', axis=0, tiled=True)  203 us
    reshape x2, local copies, waits for them, and re-layouts, shards(): split = gradient.reshape(n_rows, n_col, n_grad, piece)  110 us
    another operation x20, other arithmetic, orthonormal(): lower_factor = jnp.linalg.cholesky(gram)  103 us
    reduce_scatter x3, waiting for transfers between devices, shards(): lax.psum_scatter(jnp.dot(blocks, basis_bf, preferred_element_type=jnp.flo...  97.7 us
    dot_general x3, matrix products, sketch_of(): lax.dot_general(blocks, rows, (((0,), (0,)), ((), ())), preferred_element...  84.8 us
  transfers between devices with their start and end apart: 17, of which 16 were waited for; matrix products, arithmetic and copies ran while one was open for 3% of the time, Pallas kernels for 0%

commit v1 on v0

--- a/solution.py
+++ b/solution.py
@@ -1,3 +1,4 @@
+import functools
 import math
 import jax
 import jax.numpy as jnp
@@ -6,6 +7,45 @@
 
 FF = 53248
 POWER = 2
+
+
+def number_heaps_here(values, dim_at):
+    values = jnp.moveaxis(values, 0, dim_at)
+    block_out = values.shape
+    return values.reshape(
+        *block_out[:dim_at], block_out[dim_at] * block_out[dim_at + 1], *block_out[dim_at + 2 :]
+    )
+
+
+def _lead_shifts_all(x_local, axis_id, dim_k):
+    full_n = lax.axis_size(axis_id)
+    line_up = []
+    idx = 0
+    while idx < full_n:
+        line_up.append((idx, (idx + 1) % full_n))
+        idx += 1
+    windows = []
+    for num, ix in line_up:
+        windows.append((ix, num))
+    item_now, current_value = ([], [])
+    i = 0
+    while i < full_n - 1:
+        if i % 2 == 0:
+            item_now.append(
+                lax.ppermute(item_now[-1] if item_now else x_local, axis_name=axis_id, perm=line_up)
+            )
+        else:
+            current_value.append(
+                lax.ppermute(current_value[-1] if current_value else x_local, axis_id, windows)
+            )
+        i += 1
+    passed = jnp.stack([*item_now[::-1], x_local, *current_value], 0)
+    known = lax.axis_index(axis_id) - len(item_now)
+    passed = passed[(jnp.arange(full_n) - known) % full_n]
+    return number_heaps_here(passed, dim_k)
+
+
+column_register = functools.partial(_lead_shifts_all, axis_id="grad", dim_k=0)
 
 
 def orthonormal(rows):
@@ -51,7 +91,7 @@
         )
         if iteration < POWER:
             sketch = sketch_of(reduced.astype(jnp.bfloat16))
-    projector = lax.all_gather(basis_rows * math.sqrt(FF), "grad", axis=0, tiled=True)
+    projector = column_register(basis_rows * math.sqrt(FF))
     return (reduced, projector)
 
 

time: 2370 us -> 2430 us (1.025)
  waiting for transfers between devices: 1800 us -> 1850 us
    ppermute x0 -> x3, waiting for transfers between devices: none -> 127 us  [the longest x2 91 us: _lead_shifts_all(): lax.ppermute(item_now[-1] if item_now else x_local, axis_name=axis_id, pe...]
    all_gather x1 -> x0, waiting for transfers between devices: 49.8 us -> none  [shards(): lax.all_gather(basis_rows * math.sqrt(FF), 'grad', axis=0, tiled=True)]
    reduce_scatter x3, waiting for transfers between devices: 97.7 us -> 67.8 us  [shards(): lax.psum_scatter(jnp.dot(blocks, basis_bf, preferred_element_type=jnp.flo...]
  transfers between devices with their start and end apart: 17 -> 19, of which waited for: 16 -> 17; matrix products, arithmetic and copies ran while one was open for 3% -> 2% of each run, Pallas kernels for 0% -> 0%
where the time goes in v1:
time: 2430 us; the launch traced here: 2420 us
  waiting for transfers between devices  1850 us (76%)
  matrix products  184 us (8%)
  local copies, waits for them, and re-layouts  178 us (7%)
  other arithmetic  178 us (7%)
    all_to_all x1, waiting for transfers between devices, shards(): lax.all_to_all(split, 'grad', split_axis=2, concat_axis=0, tiled=True)  596 us
    reduce_scatter x3, waiting for transfers between devices, sketch_of(): return lax.psum_scatter(partial, 'col', scatter_dimension=0, tiled=True)  417 us
    psum x3, waiting for transfers between devices, orthonormal(): gram = lax.psum(partial_gram, ('grad', 'col'))  378 us
    all_gather x3, waiting for transfers between devices, shards(): lax.all_gather(basis_rows.astype(jnp.bfloat16), 'col', axis=0, tiled=True)  205 us
    reshape x2, local copies, waits for them, and re-layouts, shards(): split = gradient.reshape(n_rows, n_col, n_grad, piece)  110 us
    another operation x20, other arithmetic, orthonormal(): lower_factor = jnp.linalg.cholesky(gram)  103 us
    ppermute x2, waiting for transfers between devices, _lead_shifts_all(): lax.ppermute(item_now[-1] if item_now else x_local, axis_name=axis_id, pe...  91 us
    dot_general x3, matrix products, sketch_of(): lax.dot_general(blocks, rows, (((0,), (0,)), ((), ())), preferred_element...  84.8 us
  transfers between devices with their start and end apart: 19, of which 17 were waited for; matrix products, arithmetic and copies ran while one was open for 2% of the time, Pallas kernels for 0%

profile of v1, /device:TPU:0, one launch (start us, length us, event | category | flops | bytes accessed | tf_op | source)
XLA Modules:
  0.0 2421.7 jit_solution(8030043300093659749)
XLA Ops:
  7.2 73.2 %reshape.80 = bf16[512,8,4,1664]{3,2,1,0:T(4,128)(2,1)} reshape(bf16[512,53248]{1,0:T(8,128)(2,1)} %param.5) | data formatting | bytes 109051904 | tf_op jit(solution)/shard_map/reshape | solution.py:71
  80.4 36.6 %copy.11 = bf16[512,8,4,1664]{3,1,0,2:T(8,128)(2,1)} copy(bf16[512,8,4,1664]{3,2,1,0:T(4,128)(2,1)} %reshape.80) | data formatting | bytes 109051904 | tf_op jit(solution)/shard_map/reshape | solution.py:71
  117.0 12.1 all-to-all-start
  129.8 596.0 %all-to-all-done = bf16[512,8,4,1664]{3,1,0,2:T(8,128)(2,1)} async-done(((bf16[512,8,4,1664]{3,1,0,2:T(8,128)(2,1)}), bf16[512,8,4,1664]{3,1,0,2:T(8,128)(2,1)}, u32[]{:S(2)}, u32[]{:S(2)}) %all-to-all-start) | async-done | bytes 54525984 | tf_op jit(solution)/shard_map/all_to_all | solution.py:72
  725.8 36.6 %copy.23 = bf16[256,8,8,1664]{3,1,2,0:T(8,128)(2,1)} copy(bf16[256,8,8,1664]{3,2,1,0:T(8,128)(2,1)} %bitcast.43) | data formatting | bytes 109051904
  762.4 28.3 %fusion.40 = f32[13312,256]{1,0:T(8,128)} fusion(bf16[2048,13312]{1,0:T(8,128)(2,1)} %bitcast.139, bf16[2048,256]{1,0:T(8,128)(2,1)} %all-gather.7.cloned.1.call-done), kind=kOutput, calls=%fused_computation.100 | convolution fusion | flops 13958643712 | bytes 69206016 | tf_op jit(solution)/shard_map/dot_general | solution.py:77
  790.8 139.5 %reduce-scatter.7.cloned.1.call-done = f32[1664,256]{1,0:T(8,128)} async-done(((f32[13312,256]{1,0:T(8,128)}), f32[1664,256]{1,0:T(8,128)}) %reduce-scatter.7.cloned.1.call-update) | async-done | bytes 1703952 | tf_op jit(solution)/shard_map/reduce_scatter | solution.py:80
  930.3 5.8 fusion.41
  936.6 124.8 %all-reduce.5.cloned.1.call-done = f32[256,256]{0,1:T(8,128)} async-done(((f32[256,256]{0,1:T(8,128)}), f32[256,256]{0,1:T(8,128)}) %all-reduce.5.cloned.1.call-update) | async-done | bytes 262160 | tf_op jit(solution)/shard_map/psum | solution.py:59
  1063.5 11.7 cholesky.172
  1075.2 9.8 custom-call.15
  1085.6 11.7 cholesky.189
  1099.5 4.2 while.6
  1103.7 19.7 custom-call.16
  1127.9 68.2 %all-gather.9.cloned.1.call-done = bf16[13312,256]{0,1:T(8,128)(2,1)} async-done(((bf16[1664,256]{0,1:T(8,128)(2,1)}), bf16[13312,256]{0,1:T(8,128)(2,1)}) %all-gather.9.cloned.1.call-update) | async-done | bytes 6815760 | tf_op jit(solution)/shard_map/all_gather | solution.py:85
  1196.1 24.6 %convolution_bitcast_fusion.4 = f32[2048,256]{0,1:T(8,128)} fusion(bf16[13312,256]{0,1:T(8,128)(2,1)} %all-gather.9.cloned.1.call-done, bf16[2048,13312]{1,0:T(8,128)(2,1)} %bitcast.140), kind=kOutput, calls=%fused_computation.12 | convolution fusion | flops 13958643712 | bytes 63438848 | tf_op jit(solution)/shard_map/dot_general | solution.py:87
  1220.7 33.9 %reduce-scatter.9.cloned.1.call-done = f32[512,256]{0,1:T(8,128)} async-done(((f32[2048,256]{0,1:T(8,128)}), f32[512,256]{0,1:T(8,128)}) %reduce-scatter.9.cloned.1.call-update) | async-done | bytes 524304 | tf_op jit(solution)/shard_map/reduce_scatter | solution.py:86
  1256.5 26.8 %all-gather.11.cloned.1.call-done = bf16[2048,256]{0,1:T(8,128)(2,1)} async-done(((bf16[512,256]{0,1:T(8,128)(2,1)}), bf16[2048,256]{0,1:T(8,128)(2,1)}) %all-gather.11.cloned.1.call-update) | async-done | bytes 1048592 | tf_op jit(solution)/shard_map/all_gather | solution.py:76
  1283.3 28.3 %convolution_bitcast_fusion.1 = f32[13312,256]{0,1:T(8,128)} fusion(bf16[2048,256]{0,1:T(8,128)(2,1)} %all-gather.11.cloned.1.call-done, bf16[2048,13312]{1,0:T(8,128)(2,1)} %bitcast.141), kind=kOutput, calls=%fused_computation.8 | convolution fusion | flops 13958643712 | bytes 69206016 | tf_op jit(solution)/shard_map/dot_general | solution.py:77
  1311.9 138.9 %reduce-scatter.11.cloned.1.call-done = f32[1664,256]{0,1:T(8,128)} async-done(((f32[13312,256]{0,1:T(8,128)}), f32[1664,256]{0,1:T(8,128)}) %reduce-scatter.11.cloned.1.call-update) | async-done | bytes 1703952 | tf_op jit(solution)/shard_map/reduce_scatter | solution.py:80
  1450.8 4.6 fusion.42
  1455.4 126.5 %all-reduce.7.cloned.1.call-done = f32[256,256]{0,1:T(8,128)} async-done(((f32[256,256]{0,1:T(8,128)}), f32[256,256]{0,1:T(8,128)}) %all-reduce.7.cloned.1.call-update) | async-done | bytes 262160 | tf_op jit(solution)/shard_map/psum | solution.py:59
  1584.0 11.7 cholesky.206
  1595.8 9.8 custom-call.17
  1606.1 11.7 cholesky.223
  1620.5 4.5 while.7
  1625.0 19.7 custom-call.18
  1648.5 68.2 %all-gather.13.cloned.1.call-done = bf16[13312,256]{0,1:T(8,128)(2,1)} async-done(((bf16[1664,256]{0,1:T(8,128)(2,1)}), bf16[13312,256]{0,1:T(8,128)(2,1)}) %all-gather.13.cloned.1.call-update) | async-done | bytes 6815760 | tf_op jit(solution)/shard_map/all_gather | solution.py:85
  1716.6 24.6 %convolution_bitcast_fusion.3 = f32[2048,256]{0,1:T(8,128)} fusion(bf16[13312,256]{0,1:T(8,128)(2,1)} %all-gather.13.cloned.1.call-done, bf16[2048,13312]{1,0:T(8,128)(2,1)} %bitcast.142), kind=kOutput, calls=%fused_computation.11 | convolution fusion | flops 13958643712 | bytes 63438848 | tf_op jit(solution)/shard_map/dot_general | solution.py:87
  1741.3 33.9 %reduce-scatter.13.cloned.1.call-done = f32[512,256]{0,1:T(8,128)} async-done(((f32[2048,256]{0,1:T(8,128)}), f32[512,256]{0,1:T(8,128)}) %reduce-scatter.13.cloned.1.call-update) | async-done | bytes 524304 | tf_op jit(solution)/shard_map/reduce_scatter | solution.py:86
  1777.0 27.0 %all-gather.15.cloned.1.call-done = bf16[2048,256]{0,1:T(8,128)(2,1)} async-done(((bf16[512,256]{0,1:T(8,128)(2,1)}), bf16[2048,256]{0,1:T(8,128)(2,1)}) %all-gather.15.cloned.1.call-update) | async-done | bytes 1048592 | tf_op jit(solution)/shard_map/all_gather | solution.py:76
  1804.0 28.3 %convolution_bitcast_fusion = f32[13312,256]{0,1:T(8,128)} fusion(bf16[2048,256]{0,1:T(8,128)(2,1)} %all-gather.15.cloned.1.call-done, bf16[2048,13312]{1,0:T(8,128)(2,1)} %bitcast.143), kind=kOutput, calls=%fused_computation.7 | convolution fusion | flops 13958643712 | bytes 69206016 | tf_op jit(solution)/shard_map/dot_general | solution.py:77
  1832.5 139.0 %reduce-scatter.15.cloned.1.call-done = f32[1664,256]{0,1:T(8,128)} async-done(((f32[13312,256]{0,1:T(8,128)}), f32[1664,256]{0,1:T(8,128)}) %reduce-scatter.15.cloned.1.call-update) | async-done | bytes 1703952 | tf_op jit(solution)/shard_map/reduce_scatter | solution.py:80
  1971.5 4.6 fusion.43
  1976.2 126.4 %all-reduce.9.cloned.1.call-done = f32[256,256]{0,1:T(8,128)} async-done(((f32[256,256]{0,1:T(8,128)}), f32[256,256]{0,1:T(8,128)}) %all-reduce.9.cloned.1.call-update) | async-done | bytes 262160 | tf_op jit(solution)/shard_map/psum | solution.py:59
  2104.7 11.7 cholesky.240
  2116.5 9.8 custom-call.19
  2126.8 11.7 cholesky.257
  2141.1 4.2 while.8
  2145.4 19.7 custom-call.20
  2168.8 68.2 %all-gather.17.cloned.1.call-done = bf16[13312,256]{0,1:T(8,128)(2,1)} async-done(((bf16[1664,256]{0,1:T(8,128)(2,1)}), bf16[13312,256]{0,1:T(8,128)(2,1)}) %all-gather.17.cloned.1.call-update) | async-done | bytes 6815760 | tf_op jit(solution)/shard_map/all_gather | solution.py:85
  2237.0 24.6 %convolution_bitcast_fusion.2 = f32[2048,256]{0,1:T(8,128)} fusion(bf16[13312,256]{0,1:T(8,128)(2,1)} %all-gather.17.cloned.1.call-done, bf16[2048,13312]{1,0:T(8,128)(2,1)} %bitcast.144), kind=kOutput, calls=%fused_computation.10 | convolution fusion | flops 13958643712 | bytes 63438848 | tf_op jit(solution)/shard_map/dot_general | solution.py:87
  2266.6 55.1 %collective-permute-done = f32[1664,256]{0,1:T(8,128)S(1)} collective-permute-done((f32[1664,256]{0,1:T(8,128)}, f32[1664,256]{0,1:T(8,128)S(1)}, u32[]{:S(2)}, u32[]{:S(2)}) %collective-permute-start) | collective-permute-done | bytes 1703968 | tf_op jit(solution)/shard_map/ppermute | solution.py:35
  2322.3 35.9 %collective-permute-done.2 = f32[1664,256]{0,1:T(8,128)S(1)} collective-permute-done((f32[1664,256]{0,1:T(8,128)}, f32[1664,256]{0,1:T(8,128)S(1)}, u32[]{:S(2)}, u32[]{:S(2)}) %collective-permute-start.2) | collective-permute-done | bytes 1703968 | tf_op jit(solution)/shard_map/ppermute | solution.py:39
  2358.2 35.9 %collective-permute-done.1 = f32[1664,256]{0,1:T(8,128)} collective-permute-done((f32[1664,256]{0,1:T(8,128)S(1)}, f32[1664,256]{0,1:T(8,128)}, u32[]{:S(2)}, u32[]{:S(2)}) %collective-permute-start.1) | collective-permute-done | bytes 1703968 | tf_op jit(solution)/shard_map/ppermute | solution.py:35
  2394.1 4.5 pad_maximum_fusion
  2398.6 6.7 gather_fusion
  2405.3 7.6 copy.18
  (114 shorter events, 48.6 us)
Async XLA Ops:
  117.0 608.8 %all-to-all-start = ((bf16[512,8,4,1664]{3,1,0,2:T(8,128)(2,1)}), bf16[512,8,4,1664]{3,1,0,2:T(8,128)(2,1)}, u32[]{:S(2)}, u32[]{:S(2)}) async-start(bf16[512,8,4,1664]{3,1,0,2:T(8,128)(2,1)} %copy.11), calls=%async_computation | async-start | bytes 109051904 | tf_op jit(solution)/shard_map/all_to_all | solution.py:72
  129.0 633.4 %all-gather.7.cloned.1.call-start = ((), (), s32[]{:S(2)}) async-start(), calls=%async_computation.7 | async-start | bytes 1310720 | tf_op jit(solution)/shard_map/all_gather | solution.py:76
  129.8 800.5 %reduce-scatter.7.cloned.1.call-start = ((), (), s32[]{:S(2)}) async-start(), calls=%async_computation.8 | async-start | bytes 15335424 | tf_op jit(solution)/shard_map/reduce_scatter | solution.py:80
  790.7 270.7 %all-reduce.5.cloned.1.call-start = ((), (), s32[]{:S(2)}) async-start(), calls=%async_computation.9 | async-start | bytes 524288 | tf_op jit(solution)/shard_map/psum | solution.py:59
  936.1 187.3 %copy-start = (f32[1664,256]{1,0:T(8,128)S(1)}, f32[1664,256]{1,0:T(8,128)}, u32[]{:S(2)}) copy-start(f32[1664,256]{1,0:T(8,128)} %reduce-scatter.7.cloned.1.call-done) | copy-start | bytes 5111812
  936.1 260.0 %all-gather.9.cloned.1.call-start = ((), (), s32[]{:S(2)}) async-start(), calls=%async_computation.10 | async-start | bytes 7667712 | tf_op jit(solution)/shard_map/all_gather | solution.py:85
  1127.9 126.8 %reduce-scatter.9.cloned.1.call-start = ((), (), s32[]{:S(2)}) async-start(), calls=%async_computation.11 | async-start | bytes 2621440 | tf_op jit(solution)/shard_map/reduce_scatter | solution.py:86
  1220.7 62.6 %all-gather.11.cloned.1.call-start = ((), (), s32[]{:S(2)}) async-start(), calls=%async_computation.12 | async-start | bytes 1310720 | tf_op jit(solution)/shard_map/all_gather | solution.py:76
  1256.4 194.4 %reduce-scatter.11.cloned.1.call-start = ((), (), s32[]{:S(2)}) async-start(), calls=%async_computation.13 | async-start | bytes 15335424 | tf_op jit(solution)/shard_map/reduce_scatter | solution.py:80
  1311.6 270.3 %all-reduce.7.cloned.1.call-start = ((), (), s32[]{:S(2)}) async-start(), calls=%async_computation.14 | async-start | bytes 524288 | tf_op jit(solution)/shard_map/psum | solution.py:59
  1455.4 189.3 %copy-start.2 = (f32[1664,256]{0,1:T(8,128)S(1)}, f32[1664,256]{0,1:T(8,128)}, u32[]{:S(2)}) copy-start(f32[1664,256]{0,1:T(8,128)} %reduce-scatter.11.cloned.1.call-done) | copy-start | bytes 5111812
  1455.4 261.2 %all-gather.13.cloned.1.call-start = ((), (), s32[]{:S(2)}) async-start(), calls=%async_computation.15 | async-start | bytes 7667712 | tf_op jit(solution)/shard_map/all_gather | solution.py:85
  1648.4 126.8 %reduce-scatter.13.cloned.1.call-start = ((), (), s32[]{:S(2)}) async-start(), calls=%async_computation.16 | async-start | bytes 2621440 | tf_op jit(solution)/shard_map/reduce_scatter | solution.py:86
  1741.2 62.8 %all-gather.15.cloned.1.call-start = ((), (), s32[]{:S(2)}) async-start(), calls=%async_computation.17 | async-start | bytes 1310720 | tf_op jit(solution)/shard_map/all_gather | solution.py:76
  1777.0 194.5 %reduce-scatter.15.cloned.1.call-start = ((), (), s32[]{:S(2)}) async-start(), calls=%async_computation.18 | async-start | bytes 15335424 | tf_op jit(solution)/shard_map/reduce_scatter | solution.py:80
  1832.3 270.3 %all-reduce.9.cloned.1.call-start = ((), (), s32[]{:S(2)}) async-start(), calls=%async_computation.19 | async-start | bytes 524288 | tf_op jit(solution)/shard_map/psum | solution.py:59
  1976.1 189.0 %copy-start.1 = (f32[1664,256]{0,1:T(8,128)S(1)}, f32[1664,256]{0,1:T(8,128)}, u32[]{:S(2)}) copy-start(f32[1664,256]{0,1:T(8,128)} %reduce-scatter.15.cloned.1.call-done) | copy-start | bytes 5111812
  1976.1 260.9 %all-gather.17.cloned.1.call-start = ((), (), s32[]{:S(2)}) async-start(), calls=%async_computation.20 | async-start | bytes 7667712 | tf_op jit(solution)/shard_map/all_gather | solution.py:85
  2168.8 244.1 %reduce-scatter.17.cloned.1.call-start = ((), (), s32[]{:S(2)}) async-start(), calls=%async_computation.21 | async-start | bytes 2621440 | tf_op jit(solution)/shard_map/reduce_scatter | solution.py:86
  2263.6 58.0 %collective-permute-start = (f32[1664,256]{0,1:T(8,128)}, f32[1664,256]{0,1:T(8,128)S(1)}, u32[]{:S(2)}, u32[]{:S(2)}) collective-permute-start(f32[1664,256]{0,1:T(8,128)} %get-tuple-element.62), channel_id=1, source_target_pairs={{0,8},{8,16},{16,24},{24,0},{1,9},{9,17},{17,25},{25,1},{2,10},{10... | collective-permute-start | bytes 5111816 | tf_op jit(solution)/shard_map/ppermute | solution.py:35
  2265.1 93.1 %collective-permute-start.2 = (f32[1664,256]{0,1:T(8,128)}, f32[1664,256]{0,1:T(8,128)S(1)}, u32[]{:S(2)}, u32[]{:S(2)}) collective-permute-start(f32[1664,256]{0,1:T(8,128)} %get-tuple-element.62), channel_id=1, source_target_pairs={{8,0},{16,8},{24,16},{0,24},{9,1},{17,9},{25,17},{1,25},{10,2},{18... | collective-permute-start | bytes 5111816 | tf_op jit(solution)/shard_map/ppermute | solution.py:39
  2321.7 72.4 %collective-permute-start.1 = (f32[1664,256]{0,1:T(8,128)S(1)}, f32[1664,256]{0,1:T(8,128)}, u32[]{:S(2)}, u32[]{:S(2)}) collective-permute-start(f32[1664,256]{0,1:T(8,128)S(1)} %collective-permute-done), channel_id=1, source_target_pairs={{0,8},{8,16},{16,24},{24,0},{1,9},{9,17},{17,25},{25,1},{2,10},{10... | collective-permute-start | bytes 5111816 | tf_op jit(solution)/shard_map/ppermute | solution.py:35
Sparse Core Ops, SparseCore 0:
  131.7 318.6 all-gather.6
  790.8 139.4 reduce-scatter.6
  936.4 124.9 all-reduce.4
  1128.0 68.0 all-gather.8
  1220.8 33.7 reduce-scatter.8
  1256.9 26.3 all-gather.10
  1311.7 139.0 reduce-scatter.10
  1456.9 125.0 all-reduce.6
  1648.5 68.0 all-gather.12
  1741.4 33.7 reduce-scatter.12
  1777.6 26.3 all-gather.14
  1832.4 139.0 reduce-scatter.14
  1977.6 124.9 all-reduce.8
  2168.9 68.0 all-gather.16
  2261.8 51.7 reduce-scatter.16
